TPU v7x, 512 devices: a whole 4x8x8 slice. The times are simulated.
512 devices in a mesh: region: 8 (over z), dom: 64 (over y, x, core).
Axes of the slice: x: 4, y: 8, z: 8, core: 2. Of those that a mesh axis runs over, the one named last changes fastest.
Arguments:
- gauges: bfloat16 [524288, 384], P(('region', 'dom')), may hold values from -24 to 24
- couplings: bfloat16 [4096, 3, 128, 128], P(('region', 'dom')), may hold values from -0.3125 to 0.3125
- adjacency: int32 [4096, 3], P(('region', 'dom')), may hold values from 0 to 15
- send_list: int32 [1024], P(('region', 'dom')), may hold values from 0 to 7
- coverage: int32 [4096, 2], P(('region', 'dom')), may hold values from 0 to 4
- positive: int32 [524288], P(('region', 'dom')), may hold values from 0 to 255
- patches: bfloat16 [65536, 512], P(('region', 'dom')), may hold values from -24 to 24
- message_weight: bfloat16 [384, 384], replicated, may hold values from -0.3125 to 0.3125
- self_weight: bfloat16 [384, 384], replicated, may hold values from -0.3125 to 0.3125
- output_weight: bfloat16 [384, 512], replicated, may hold values from -0.3125 to 0.3125
- patch_weight: bfloat16 [512, 512], replicated, may hold values from -0.25 to 0.25
Outputs:
- grad_message: bfloat16 [384, 384], P('dom')
- grad_self: bfloat16 [384, 384], P('dom')
- grad_output: bfloat16 [384, 512], P('dom')
- grad_patch: bfloat16 [512, 512], P('dom')
Inputs may be any that keep to these rules, and one draw needn't show every extreme that they name: `adjacency`: indexes the partition's block table of 16 entries. `send_list`: indexes the partition's own blocks. `coverage`: indexes the partition's patch table of 5 entries.
All inputs are finite; a program needn't handle non-finite values.
Results may differ from a plain program's by a relative error of at most 0.015.
Values may be sent and summed in bfloat16 or wider, within the bound.
No kernel may reach another device: no remote copies, remote signals or barrier semaphores. Data moves between devices by JAX's collectives and lax.ppermute only.
A program may use at most 64 MiB of HBM per device.

v0:
```python
import math
import jax
import jax.numpy as jnp
from jax import lax
from jax.sharding import PartitionSpec as P

BLOCK = 128
loss_gain = 16.0
offsets_by = (1, 2, -1, -2)


def passed_along(shard, axis, by):
    count = lax.axis_size(axis)
    return lax.ppermute(shard, axis, [(i, (i + by) % count) for i in range(count)])


def silu_slope(argument):
    sigmoid_v = jax.nn.sigmoid(argument)
    return sigmoid_v * (1.0 + argument * (1.0 - sigmoid_v))


def boundary_table(blocks, send_list):
    outgoing = blocks[send_list]
    pieces = [blocks]
    for step_by in offsets_by:
        pieces.append(passed_along(outgoing, "dom", step_by))
    return jnp.concatenate(pieces, axis=0)


def patch_table_near(patch_blocks):
    pieces = [patch_blocks]
    for step_by in offsets_by:
        pieces.append(passed_along(patch_blocks, "dom", step_by))
    return jnp.concatenate(pieces, axis=0)


def shards(
    gauges,
    couplings,
    adjacency,
    send_list,
    coverage,
    positive,
    patches,
    message_weight,
    self_weight,
    output_weight,
    patch_weight,
):
    f32 = jnp.float32
    bf16 = jnp.bfloat16
    width = gauges.shape[1]
    wide = patches.shape[1]
    count = couplings.shape[0]
    blocks = gauges.reshape(count, BLOCK, width)
    block_table = boundary_table(blocks, send_list)
    picked = block_table[adjacency]
    message = (
        jnp.einsum("bkij,bkjd->bid", couplings, picked, preferred_element_type=f32)
        .astype(bf16)
        .reshape(-1, width)
    )
    pre_act = jnp.dot(message, message_weight, preferred_element_type=f32) + jnp.dot(
        gauges, self_weight, preferred_element_type=f32
    )
    hidden = (gauges.astype(f32) + jax.nn.silu(pre_act)).astype(bf16)
    queries = jnp.dot(hidden, output_weight, preferred_element_type=f32).astype(bf16)
    patch_blocks = patches.reshape(-1, BLOCK, wide)
    covered = patch_table_near(patch_blocks)[coverage]
    flat_cover = covered.reshape(-1, wide)
    key_rows = (
        jnp.dot(flat_cover, patch_weight, preferred_element_type=f32)
        .astype(bf16)
        .reshape(count, -1, wide)
    )
    query_blocks = queries.reshape(count, BLOCK, wide)
    inv_root = 1.0 / math.sqrt(wide)
    logits = (
        jnp.einsum("bie,bje->bij", query_blocks, key_rows, preferred_element_type=f32) * inv_root
    )
    soft = jax.nn.softmax(logits, axis=-1)
    columns = jnp.arange(logits.shape[2], dtype=jnp.int32)
    target = (positive.reshape(count, BLOCK)[:, :, None] == columns).astype(f32)
    total_gauges = gauges.shape[0] * lax.axis_size("region") * lax.axis_size("dom")
    loss_scale = loss_gain / math.sqrt(total_gauges)
    logit_grad = ((soft - target) * loss_scale).astype(bf16)
    query_grad = (
        (jnp.einsum("bij,bje->bie", logit_grad, key_rows, preferred_element_type=f32) * inv_root)
        .astype(bf16)
        .reshape(-1, wide)
    )
    key_grad = (
        (
            jnp.einsum("bij,bie->bje", logit_grad, query_blocks, preferred_element_type=f32)
            * inv_root
        )
        .astype(bf16)
        .reshape(-1, wide)
    )
    grad_patch = jnp.dot(flat_cover.T, key_grad, preferred_element_type=f32)
    grad_output = jnp.dot(hidden.T, query_grad, preferred_element_type=f32)
    hidden_grad = jnp.dot(query_grad, output_weight.T, preferred_element_type=f32)
    act_grad = (hidden_grad * silu_slope(pre_act)).astype(bf16)
    grad_message = jnp.dot(message.T, act_grad, preferred_element_type=f32)
    grad_self = jnp.dot(gauges.T, act_grad, preferred_element_type=f32)
    summed = (
        lax.psum(grad_message.astype(jnp.bfloat16), "region").astype(jnp.float32),
        lax.psum(grad_self.astype(jnp.bfloat16), "region").astype(jnp.float32),
        lax.psum(grad_output.astype(jnp.bfloat16), "region").astype(jnp.float32),
        lax.psum(grad_patch.astype(jnp.bfloat16), "region").astype(jnp.float32),
    )
    shares = (
        lax.psum_scatter(summed[0], "dom", scatter_dimension=0, tiled=True),
        lax.psum_scatter(summed[1], "dom", scatter_dimension=0, tiled=True),
        lax.psum_scatter(summed[2], "dom", scatter_dimension=0, tiled=True),
        lax.psum_scatter(summed[3], "dom", scatter_dimension=0, tiled=True),
    )
    return (
        shares[0].astype(bf16),
        shares[1].astype(bf16),
        shares[2].astype(bf16),
        shares[3].astype(bf16),
    )


def solution(mesh):
    placed = (
        P(("region", "dom"), None),
        P(("region", "dom"), None, None, None),
        P(("region", "dom"), None),
        P(("region", "dom")),
        P(("region", "dom"), None),
        P(("region", "dom")),
        P(("region", "dom"), None),
        P(),
        P(),
        P(),
        P(),
    )
    return jax.shard_map(
        shards,
        mesh=mesh,
        in_specs=placed,
        out_specs=(P("dom", None), P("dom", None), P("dom", None), P("dom", None)),
        check_vma=False,
    )
```

profile of v0, /device:TPU:25, one launch (start us, length us, event | category | flops | bytes accessed | tf_op | source)
XLA Modules:
  0.0 390.5 jit_solution(838861163296844405)
XLA Ops:
  7.2 0.0 copy-start
  7.2 0.0 copy-start.10
  7.2 0.0 copy-start.11
  7.2 0.0 copy-start.12
  7.2 0.0 all-reduce.11.cloned.1.call-start
  7.3 0.7 compare_select_fusion.2
  8.0 2.4 gather_fusion
  10.4 3.7 collective-permute-start
  14.1 3.1 collective-permute-start.1
  17.2 1.9 collective-permute-start.2
  19.1 3.6 collective-permute-start.4
  22.8 2.8 collective-permute-start.5
  25.6 2.1 constant_dynamic-update-slice_fusion.4
  27.7 0.9 constant_dynamic-update-slice_fusion.9
  28.7 0.1 copy.23
  28.7 0.1 reshape.53
  28.8 0.1 copy.24
  28.9 0.1 reshape.61
  29.0 0.0 collective-permute-done.4
  29.0 3.4 collective-permute-start.6
  32.4 0.5 collective-permute-done.5
  32.9 3.9 %collective-permute-start.7 = (bf16[1,128,512]{2,1,0:T(8,128)(2,1)S(1)}, bf16[1,128,512]{2,1,0:T(8,128)(2,1)S(1)}, u32[]{:S(2)}, u32[]{:S(2)}) collective-permute-start(bf16[1,128,512]{2,1,0:T(8,128)(2,1)S(1)} %bitcast.60), channel_id=1, source_target_pairs={{0,62},{1,63},{2,0},{3,1},{4,2},{5,3},{6,4},{7,5},{8,6},{9,7},{10,... | collective-permute-start | bytes 393224 | tf_op jit(solution)/shard_map/ppermute | solution.py:14
  36.9 0.0 collective-permute-done.6
  36.9 6.0 %collective-permute-start.3 = (bf16[2,128,384]{2,1,0:T(8,128)(2,1)}, bf16[2,128,384]{2,1,0:T(8,128)(2,1)}, u32[]{:S(2)}, u32[]{:S(2)}) collective-permute-start(bf16[2,128,384]{2,1,0:T(8,128)(2,1)} %gather_fusion), channel_id=1, source_target_pairs={{0,62},{1,63},{2,0},{3,1},{4,2},{5,3},{6,4},{7,5},{8,6},{9,7},{10,... | collective-permute-start | bytes 589832 | tf_op jit(solution)/shard_map/ppermute | solution.py:14
  42.9 0.0 collective-permute-done.7
  43.0 0.7 gather_fusion.2
  43.7 4.0 %convolution_convert_fusion = bf16[2048,512]{1,0:T(8,128)(2,1)} fusion(bf16[2048,512]{1,0:T(8,128)(2,1)S(1)} %bitcast.48, bf16[512,512]{1,0:T(8,128)(2,1)} %param.21), kind=kOutput, calls=%fused_computation.6 | convolution fusion | flops 1074790400 | bytes 4718592 | tf_op jit(solution)/shard_map/dot_general | solution.py:72
  47.7 0.0 collective-permute-done
  47.7 1.6 constant_dynamic-update-slice_fusion.3
  49.3 0.0 collective-permute-done.1
  49.3 1.6 constant_dynamic-update-slice_fusion.2
  50.9 0.0 collective-permute-done.2
  50.9 1.6 constant_dynamic-update-slice_fusion.1
  52.6 0.0 collective-permute-done.3
  52.6 1.6 constant_dynamic-update-slice_fusion
  54.2 2.5 gather_fusion.1
  56.7 0.0 copy-start.9
  56.7 0.7 bitcast_convert_fusion
  57.4 0.0 copy-start.5
  57.4 0.0 copy-start.13
  57.5 0.2 copy-done.9
  57.7 0.6 fusion.19
  58.3 0.6 copy-done.5
  58.9 0.1 copy-done.13
  58.9 2.0 add_convert_fusion
  61.0 0.7 convolution_convert_fusion.1
  61.7 5.9 %multiply_convert_fusion.1 = bf16[8,128,512]{2,1,0:T(8,128)(2,1)} fusion(bf16[8,256,512]{2,1,0:T(8,128)(2,1)} %bitcast.63, s32[8,128]{1,0:T(8,128)S(1)} %bitcast.61, bf16[8,128,512]{2,1,0:T(8,128)(2,1)S(1)} %bitcast.55), kind=kOutput, calls=%fused_computation.7 | convolution fusion | flops 540019200 | bytes 4198400 | tf_op jit(solution)/shard_map/bij,bje->bie/dot_general | solution.py:88
  67.6 2.7 convolution_convert_fusion.3
  70.3 2.4 multiply_convert_fusion.2
  72.7 1.3 convolution_convert_fusion.5
  74.0 1.3 fusion.8
  75.3 6.1 %multiply_convert_fusion = bf16[8,256,512]{2,1,0:T(8,128)(2,1)} fusion(bf16[8,128,512]{2,1,0:T(8,128)(2,1)} %bitcast.56, s32[8,128]{1,0:T(8,128)S(1)} %bitcast.62, bf16[8,256,512]{2,1,0:T(8,128)(2,1)} %bitcast.64), kind=kOutput, calls=%fused_computation.5 | convolution fusion | flops 541067776 | bytes 5246976 | tf_op jit(solution)/shard_map/bij,bie->bje/dot_general | solution.py:94
  81.4 3.7 convolution_convert_fusion.2
  85.1 0.0 all-reduce.11.cloned.1.call-update
  85.1 0.0 all-reduce.9.cloned.1.call-start
  85.1 86.3 %all-reduce.11.cloned.1.call-done = (bf16[384,384]{1,0:T(8,128)(2,1)}, bf16[384,384]{0,1:T(8,128)(2,1)}, bf16[384,512]{1,0:T(8,128)(2,1)}, bf16[512,512]{1,0:T(8,128)(2,1)}) async-done(((bf16[384,384]{1,0:T(8,128)(2,1)}, bf16[384,384]{0,1:T(8,128)(2,1)}, bf16[384,512]{1,0:T(8,128)(2,1)}, bf16[512,512]{1,0:T(8,128)(2,1)}), (bf16[384,384]{1,0:T(8,128)(2,1)}, bf16[384,384]{0,1:T(8,128)(2,1)}, ...) | async-done | bytes 1507344 | tf_op jit(solution)/shard_map/psum | solution.py:107
  171.5 0.0 all-reduce.9.cloned.1.call-update
  171.5 1.3 dynamic-slice
  174.1 203.9 %all-reduce.9.cloned.1.call-done = (bf16[384,384]{1,0:T(8,128)(2,1)}, bf16[384,384]{0,1:T(8,128)(2,1)}, bf16[384,512]{1,0:T(8,128)(2,1)}, bf16[512,512]{1,0:T(8,128)(2,1)}) async-done(((bf16[384,384]{1,0:T(8,128)(2,1)}, bf16[384,384]{0,1:T(8,128)(2,1)}, bf16[384,512]{1,0:T(8,128)(2,1)}, bf16[512,512]{1,0:T(8,128)(2,1)}), (bf16[384,384]{1,0:T(8,128)(2,1)}, bf16[384,384]{0,1:T(8,128)(2,1)}, ...) | async-done | bytes 1507344
  378.0 1.0 dynamic-slice_convert_fusion
  379.0 0.7 copy.26
  379.7 1.3 dynamic-slice_convert_fusion.2
  381.0 1.3 dynamic-slice_convert_fusion.3
  382.3 1.3 dynamic-slice_convert_fusion.1
  (31 shorter events, 0.1 us)
Async XLA Ops:
  7.2 49.6 %copy-start = (bf16[8,3,128,128]{3,2,1,0:T(8,128)(2,1)S(1)}, bf16[8,3,128,128]{3,2,1,0:T(8,128)(2,1)}, u32[]{:S(2)}) copy-start(bf16[8,3,128,128]{3,2,1,0:T(8,128)(2,1)} %param.12) | copy-start | bytes 2359300
  7.2 21.8 %copy-start.10 = (bf16[128,512]{1,0:T(8,128)(2,1)S(1)}, bf16[128,512]{1,0:T(8,128)(2,1)}, u32[]{:S(2)}) copy-start(bf16[128,512]{1,0:T(8,128)(2,1)} %param.17) | copy-start | bytes 393220
  7.2 21.4 %copy-start.11 = (s32[8,3]{0,1:T(4,128)S(1)}, s32[8,3]{0,1:T(4,128)}, u32[]{:S(2)}) copy-start(s32[8,3]{0,1:T(4,128)} %param.13) | copy-start | bytes 292
  7.2 21.6 %copy-start.12 = (s32[8,2]{0,1:T(2,128)S(1)}, s32[8,2]{0,1:T(2,128)}, u32[]{:S(2)}) copy-start(s32[8,2]{0,1:T(2,128)} %param.15) | copy-start | bytes 196
  7.2 164.2 %all-reduce.11.cloned.1.call-start = ((), (), s32[]{:S(2)}) async-start(), calls=%async_computation.1 | async-start | bytes 3014656 | tf_op jit(solution)/shard_map/psum | solution.py:107
  10.4 37.3 %collective-permute-start = (bf16[2,128,384]{2,1,0:T(8,128)(2,1)}, bf16[2,128,384]{2,1,0:T(8,128)(2,1)}, u32[]{:S(2)}, u32[]{:S(2)}) collective-permute-start(bf16[2,128,384]{2,1,0:T(8,128)(2,1)} %gather_fusion), channel_id=1, source_target_pairs={{0,1},{1,2},{2,3},{3,4},{4,5},{5,6},{6,7},{7,8},{8,9},{9,10},{10,1... | collective-permute-start | bytes 589832 | tf_op jit(solution)/shard_map/ppermute | solution.py:14
  14.1 35.2 %collective-permute-start.1 = (bf16[2,128,384]{2,1,0:T(8,128)(2,1)}, bf16[2,128,384]{2,1,0:T(8,128)(2,1)}, u32[]{:S(2)}, u32[]{:S(2)}) collective-permute-start(bf16[2,128,384]{2,1,0:T(8,128)(2,1)} %gather_fusion), channel_id=1, source_target_pairs={{0,2},{1,3},{2,4},{3,5},{4,6},{5,7},{6,8},{7,9},{8,10},{9,11},{10,... | collective-permute-start | bytes 589832 | tf_op jit(solution)/shard_map/ppermute | solution.py:14
  17.2 33.7 %collective-permute-start.2 = (bf16[2,128,384]{2,1,0:T(8,128)(2,1)}, bf16[2,128,384]{2,1,0:T(8,128)(2,1)}, u32[]{:S(2)}, u32[]{:S(2)}) collective-permute-start(bf16[2,128,384]{2,1,0:T(8,128)(2,1)} %gather_fusion), channel_id=1, source_target_pairs={{0,63},{1,0},{2,1},{3,2},{4,3},{5,4},{6,5},{7,6},{8,7},{9,8},{10,9... | collective-permute-start | bytes 589832 | tf_op jit(solution)/shard_map/ppermute | solution.py:14
  19.1 9.9 %collective-permute-start.4 = (bf16[1,128,512]{2,1,0:T(8,128)(2,1)}, bf16[1,128,512]{2,1,0:T(8,128)(2,1)S(1)}, u32[]{:S(2)}, u32[]{:S(2)}) collective-permute-start(bf16[1,128,512]{2,1,0:T(8,128)(2,1)} %bitcast.57), channel_id=1, source_target_pairs={{0,1},{1,2},{2,3},{3,4},{4,5},{5,6},{6,7},{7,8},{8,9},{9,10},{10,1... | collective-permute-start | bytes 393224 | tf_op jit(solution)/shard_map/ppermute | solution.py:14
  22.8 10.1 %collective-permute-start.5 = (bf16[1,128,512]{2,1,0:T(8,128)(2,1)}, bf16[1,128,512]{2,1,0:T(8,128)(2,1)S(1)}, u32[]{:S(2)}, u32[]{:S(2)}) collective-permute-start(bf16[1,128,512]{2,1,0:T(8,128)(2,1)} %bitcast.58), channel_id=1, source_target_pairs={{0,2},{1,3},{2,4},{3,5},{4,6},{5,7},{6,8},{7,9},{8,10},{9,11},{10,... | collective-permute-start | bytes 393224 | tf_op jit(solution)/shard_map/ppermute | solution.py:14
  29.0 7.8 %collective-permute-start.6 = (bf16[1,128,512]{2,1,0:T(8,128)(2,1)S(1)}, bf16[1,128,512]{2,1,0:T(8,128)(2,1)S(1)}, u32[]{:S(2)}, u32[]{:S(2)}) collective-permute-start(bf16[1,128,512]{2,1,0:T(8,128)(2,1)S(1)} %bitcast.59), channel_id=1, source_target_pairs={{0,63},{1,0},{2,1},{3,2},{4,3},{5,4},{6,5},{7,6},{8,7},{9,8},{10,9... | collective-permute-start | bytes 393224 | tf_op jit(solution)/shard_map/ppermute | solution.py:14
  32.9 10.0 %collective-permute-start.7 = (bf16[1,128,512]{2,1,0:T(8,128)(2,1)S(1)}, bf16[1,128,512]{2,1,0:T(8,128)(2,1)S(1)}, u32[]{:S(2)}, u32[]{:S(2)}) collective-permute-start(bf16[1,128,512]{2,1,0:T(8,128)(2,1)S(1)} %bitcast.60), channel_id=1, source_target_pairs={{0,62},{1,63},{2,0},{3,1},{4,2},{5,3},{6,4},{7,5},{8,6},{9,7},{10,... | collective-permute-start | bytes 393224 | tf_op jit(solution)/shard_map/ppermute | solution.py:14
  36.9 15.7 %collective-permute-start.3 = (bf16[2,128,384]{2,1,0:T(8,128)(2,1)}, bf16[2,128,384]{2,1,0:T(8,128)(2,1)}, u32[]{:S(2)}, u32[]{:S(2)}) collective-permute-start(bf16[2,128,384]{2,1,0:T(8,128)(2,1)} %gather_fusion), channel_id=1, source_target_pairs={{0,62},{1,63},{2,0},{3,1},{4,2},{5,3},{6,4},{7,5},{8,6},{9,7},{10,... | collective-permute-start | bytes 589832 | tf_op jit(solution)/shard_map/ppermute | solution.py:14
  43.6 4.0 %copy-start.1 = (bf16[16,128,512]{2,1,0:T(8,128)(2,1)}, bf16[16,128,512]{2,1,0:T(8,128)(2,1)S(1)}, u32[]{:S(2)}) copy-start(bf16[16,128,512]{2,1,0:T(8,128)(2,1)S(1)} %gather_fusion.2) | copy-start | bytes 6291460
  56.7 1.0 copy-start.9
  57.4 3.5 copy-start.3
  57.4 1.4 copy-start.5
  57.4 1.5 copy-start.13
  58.9 2.0 copy-start.7
  61.0 0.7 copy-start.14
  61.7 5.9 %copy-start.6 = (bf16[1024,512]{1,0:T(8,128)(2,1)}, bf16[1024,512]{1,0:T(8,128)(2,1)S(1)}, u32[]{:S(2)}) copy-start(bf16[1024,512]{1,0:T(8,128)(2,1)S(1)} %convolution_convert_fusion.1) | copy-start | bytes 3145732
  67.6 2.7 copy-start.8
  67.6 2.7 copy-start.15
  70.3 2.4 copy-start.4
  75.3 6.1 %copy-start.2 = (bf16[16,128,512]{2,1,0:T(8,128)(2,1)S(1)}, bf16[16,128,512]{2,1,0:T(8,128)(2,1)}, u32[]{:S(2)}) copy-start(bf16[16,128,512]{2,1,0:T(8,128)(2,1)} %copy-done.1) | copy-start | bytes 6291460
  85.1 292.9 %all-reduce.9.cloned.1.call-start = ((), (), s32[]{:S(2)}) async-start(), calls=%async_computation | async-start | bytes 3014656
Sparse Core Ops, SparseCore 0:
  85.2 86.2 all-reduce.10
  175.2 202.7 all-reduce.8
where the time goes:
time: 391 us; the launch traced here: 390 us
  waiting for transfers between devices  291 us (74%)
  matrix products  31.3 us (8%)
  starting transfers between devices  28.6 us (7%)
  local copies, waits for them, and re-layouts  23.3 us (6%)
  between operations  15.7 us (4%)
    unnamed x3, waiting for transfers between devices  204 us
    psum x1, waiting for transfers between devices, shards(): lax.psum(grad_message.astype(jnp.bfloat16), 'region').astype(jnp.float32)  86.3 us
    ppermute x8, starting transfers between devices, passed_along(): lax.ppermute(shard, axis, [(i, (i + by) % count) for i in range(count)])  28.5 us
    unnamed x42, local copies, waits for them, and re-layouts  10.8 us
  transfers between devices with their start and end apart: 10, of which 3 were waited for; matrix products, arithmetic and copies ran while one was open for 4% of the time, Pallas kernels for 0%

commit v1 on v0

--- a/solution.py
+++ b/solution.py
@@ -104,7 +104,9 @@
     grad_message = jnp.dot(message.T, act_grad, preferred_element_type=f32)
     grad_self = jnp.dot(gauges.T, act_grad, preferred_element_type=f32)
     summed = (
-        lax.psum(grad_message.astype(jnp.bfloat16), "region").astype(jnp.float32),
+        jnp.sum(lax.all_gather(grad_message.astype(jnp.bfloat16), "region"), axis=0).astype(
+            jnp.float32
+        ),
         lax.psum(grad_self.astype(jnp.bfloat16), "region").astype(jnp.float32),
         lax.psum(grad_output.astype(jnp.bfloat16), "region").astype(jnp.float32),
         lax.psum(grad_patch.astype(jnp.bfloat16), "region").astype(jnp.float32),

time: 391 us -> 423 us (1.082)
  waiting for transfers between devices: 291 us -> 318 us
    all_gather x0 -> x1, waiting for transfers between devices: none -> 33.4 us  [shards(): lax.all_gather(grad_message.astype(jnp.bfloat16), 'region')]
    psum x1, waiting for transfers between devices: 86.3 us -> 80.1 us  [shards(): lax.psum(grad_self.astype(jnp.bfloat16), 'region').astype(jnp.float32)]
    unnamed x3 -> x4, waiting for transfers between devices: 204 us -> 204 us
  transfers between devices with their start and end apart: 10 -> 11, of which waited for: 3 -> 4; matrix products, arithmetic and copies ran while one was open for 4% -> 7% of each run, Pallas kernels for 0% -> 0%
where the time goes in v1:
time: 423 us; the launch traced here: 422 us
  waiting for transfers between devices  318 us (75%)
  matrix products  31.6 us (7%)
  starting transfers between devices  28.6 us (7%)
  local copies, waits for them, and re-layouts  24.3 us (6%)
  between operations  15.4 us (4%)
    unnamed x4, waiting for transfers between devices  204 us
    psum x1, waiting for transfers between devices, shards(): lax.psum(grad_self.astype(jnp.bfloat16), 'region').astype(jnp.float32)  80.1 us
    all_gather x1, waiting for transfers between devices, shards(): lax.all_gather(grad_message.astype(jnp.bfloat16), 'region')  33.4 us
    ppermute x8, starting transfers between devices, passed_along(): lax.ppermute(shard, axis, [(i, (i + by) % count) for i in range(count)])  28.5 us
    unnamed x42, local copies, waits for them, and re-layouts  11.8 us
  transfers between devices with their start and end apart: 11, of which 4 were waited for; matrix products, arithmetic and copies ran while one was open for 7% of the time, Pallas kernels for 0%

profile of v1, /device:TPU:25, one launch (start us, length us, event | category | flops | bytes accessed | tf_op | source)
XLA Modules:
  0.0 421.7 jit_solution(5065816820308573451)
XLA Ops:
  7.2 0.0 copy-start
  7.2 0.0 copy-start.9
  7.2 0.0 all-gather.3.cloned.1.call-start
  7.3 0.7 compare_select_fusion.2
  8.0 2.4 gather_fusion
  10.4 3.7 collective-permute-start
  14.1 3.1 collective-permute-start.1
  17.2 1.9 collective-permute-start.2
  19.1 3.6 collective-permute-start.4
  22.8 2.8 collective-permute-start.5
  25.6 2.1 constant_dynamic-update-slice_fusion.4
  27.7 0.9 constant_dynamic-update-slice_fusion.9
  28.7 0.1 copy.23
  28.7 0.1 reshape.53
  28.8 0.1 copy.24
  28.9 0.1 reshape.61
  29.0 0.0 collective-permute-done.4
  29.0 3.3 collective-permute-start.6
  32.4 0.5 collective-permute-done.5
  32.9 4.0 collective-permute-start.7
  36.9 0.0 collective-permute-done.6
  36.9 6.0 %collective-permute-start.3 = (bf16[2,128,384]{2,1,0:T(8,128)(2,1)}, bf16[2,128,384]{2,1,0:T(8,128)(2,1)}, u32[]{:S(2)}, u32[]{:S(2)}) collective-permute-start(bf16[2,128,384]{2,1,0:T(8,128)(2,1)} %gather_fusion), channel_id=1, source_target_pairs={{0,62},{1,63},{2,0},{3,1},{4,2},{5,3},{6,4},{7,5},{8,6},{9,7},{10,... | collective-permute-start | bytes 589832 | tf_op jit(solution)/shard_map/ppermute | solution.py:14
  42.9 0.0 collective-permute-done.7
  42.9 0.7 gather_fusion.2
  43.6 4.1 convolution_convert_fusion
  47.7 0.0 collective-permute-done
  47.7 1.6 constant_dynamic-update-slice_fusion.3
  49.3 1.6 constant_dynamic-update-slice_fusion.2
  51.0 1.6 constant_dynamic-update-slice_fusion.1
  52.6 1.6 constant_dynamic-update-slice_fusion
  54.2 2.5 gather_fusion.1
  56.8 0.0 copy-start.8
  56.8 0.7 bitcast_convert_fusion
  57.5 0.0 copy-start.5
  57.5 0.0 copy-start.12
  57.5 0.2 copy-done.8
  57.7 0.6 fusion.19
  58.3 0.6 copy-done.5
  58.9 0.1 copy-done.12
  59.0 2.0 add_convert_fusion
  61.0 0.7 convolution_convert_fusion.1
  61.7 5.8 %multiply_convert_fusion.1 = bf16[8,128,512]{2,1,0:T(8,128)(2,1)} fusion(bf16[8,256,512]{2,1,0:T(8,128)(2,1)} %bitcast.65, s32[8,128]{1,0:T(8,128)S(1)} %bitcast.63, bf16[8,128,512]{2,1,0:T(8,128)(2,1)S(1)} %bitcast.57), kind=kOutput, calls=%fused_computation.7 | convolution fusion | flops 540019200 | bytes 4198400 | tf_op jit(solution)/shard_map/bij,bje->bie/dot_general | solution.py:88
  67.5 2.9 multiply_convert_fusion.2
  70.4 0.9 copy-done.15
  71.3 1.3 convolution_convert_fusion.5
  72.7 0.0 all-gather.3.cloned.1.call-update
  72.7 0.0 all-reduce.11.cloned.1.call-start
  72.7 2.5 fusion.8
  75.2 1.3 convolution_convert_fusion.3
  76.5 6.1 %multiply_convert_fusion = bf16[8,256,512]{2,1,0:T(8,128)(2,1)} fusion(bf16[8,128,512]{2,1,0:T(8,128)(2,1)} %bitcast.58, s32[8,128]{1,0:T(8,128)S(1)} %bitcast.64, bf16[8,256,512]{2,1,0:T(8,128)(2,1)} %bitcast.66), kind=kOutput, calls=%fused_computation.5 | convolution fusion | flops 541067776 | bytes 5246976 | tf_op jit(solution)/shard_map/bij,bie->bje/dot_general | solution.py:94
  82.6 3.7 convolution_convert_fusion.2
  86.3 0.0 all-reduce.11.cloned.1.call-update
  86.3 0.0 all-reduce.9.cloned.1.call-start
  86.4 33.4 %all-gather.3.cloned.1.call-done = bf16[3072,384]{1,0:T(8,128)(2,1)} async-done(((bf16[384,384]{1,0:T(8,128)(2,1)}), bf16[3072,384]{1,0:T(8,128)(2,1)}) %all-gather.3.cloned.1.call-update) | async-done | bytes 2359312 | tf_op jit(solution)/shard_map/all_gather | solution.py:107
  119.7 2.8 reduce_sum.22
  122.5 80.1 %all-reduce.11.cloned.1.call-done = (bf16[384,384]{0,1:T(8,128)(2,1)}, bf16[384,512]{1,0:T(8,128)(2,1)}, bf16[512,512]{1,0:T(8,128)(2,1)}) async-done(((bf16[384,384]{0,1:T(8,128)(2,1)}, bf16[384,512]{1,0:T(8,128)(2,1)}, bf16[512,512]{1,0:T(8,128)(2,1)}), (bf16[384,384]{0,1:T(8,128)(2,1)}, bf16[384,512]{1,0:T(8,128)(2,1)}, bf16[512,512]{1,0:T(8,128)(2,1)})) %all-reduce.11.cloned.1.call-update) | async-done | bytes 1212432 | tf_op jit(solution)/shard_map/psum | solution.py:110
  202.6 0.0 all-reduce.9.cloned.1.call-update
  202.6 1.3 dynamic-slice
  205.2 204.4 %all-reduce.9.cloned.1.call-done = (bf16[384,384]{1,0:T(8,128)(2,1)}, bf16[384,384]{0,1:T(8,128)(2,1)}, bf16[384,512]{1,0:T(8,128)(2,1)}, bf16[512,512]{1,0:T(8,128)(2,1)}) async-done(((bf16[384,384]{1,0:T(8,128)(2,1)}, bf16[384,384]{0,1:T(8,128)(2,1)}, bf16[384,512]{1,0:T(8,128)(2,1)}, bf16[512,512]{1,0:T(8,128)(2,1)}), (bf16[384,384]{1,0:T(8,128)(2,1)}, bf16[384,384]{0,1:T(8,128)(2,1)}, ...) | async-done | bytes 1507344
  409.6 1.0 dynamic-slice_convert_fusion
  410.6 0.7 copy.26
  411.3 1.3 dynamic-slice_convert_fusion.2
  412.6 1.3 dynamic-slice_convert_fusion.3
  413.9 1.3 dynamic-slice_convert_fusion.1
  (35 shorter events, 0.1 us)
Async XLA Ops:
  7.2 49.6 %copy-start = (bf16[8,3,128,128]{3,2,1,0:T(8,128)(2,1)S(1)}, bf16[8,3,128,128]{3,2,1,0:T(8,128)(2,1)}, u32[]{:S(2)}) copy-start(bf16[8,3,128,128]{3,2,1,0:T(8,128)(2,1)} %param.12) | copy-start | bytes 2359300
  7.2 21.8 %copy-start.9 = (bf16[128,512]{1,0:T(8,128)(2,1)S(1)}, bf16[128,512]{1,0:T(8,128)(2,1)}, u32[]{:S(2)}) copy-start(bf16[128,512]{1,0:T(8,128)(2,1)} %param.17) | copy-start | bytes 393220
  7.2 21.4 %copy-start.10 = (s32[8,3]{0,1:T(4,128)S(1)}, s32[8,3]{0,1:T(4,128)}, u32[]{:S(2)}) copy-start(s32[8,3]{0,1:T(4,128)} %param.13) | copy-start | bytes 292
  7.2 21.6 %copy-start.11 = (s32[8,2]{0,1:T(2,128)S(1)}, s32[8,2]{0,1:T(2,128)}, u32[]{:S(2)}) copy-start(s32[8,2]{0,1:T(2,128)} %param.15) | copy-start | bytes 196
  7.2 112.5 %all-gather.3.cloned.1.call-start = ((), (), s32[]{:S(2)}) async-start(), calls=%async_computation | async-start | bytes 2654208 | tf_op jit(solution)/shard_map/all_gather | solution.py:107
  10.4 37.3 %collective-permute-start = (bf16[2,128,384]{2,1,0:T(8,128)(2,1)}, bf16[2,128,384]{2,1,0:T(8,128)(2,1)}, u32[]{:S(2)}, u32[]{:S(2)}) collective-permute-start(bf16[2,128,384]{2,1,0:T(8,128)(2,1)} %gather_fusion), channel_id=1, source_target_pairs={{0,1},{1,2},{2,3},{3,4},{4,5},{5,6},{6,7},{7,8},{8,9},{9,10},{10,1... | collective-permute-start | bytes 589832 | tf_op jit(solution)/shard_map/ppermute | solution.py:14
  14.1 35.3 %collective-permute-start.1 = (bf16[2,128,384]{2,1,0:T(8,128)(2,1)}, bf16[2,128,384]{2,1,0:T(8,128)(2,1)}, u32[]{:S(2)}, u32[]{:S(2)}) collective-permute-start(bf16[2,128,384]{2,1,0:T(8,128)(2,1)} %gather_fusion), channel_id=1, source_target_pairs={{0,2},{1,3},{2,4},{3,5},{4,6},{5,7},{6,8},{7,9},{8,10},{9,11},{10,... | collective-permute-start | bytes 589832 | tf_op jit(solution)/shard_map/ppermute | solution.py:14
  17.2 33.8 %collective-permute-start.2 = (bf16[2,128,384]{2,1,0:T(8,128)(2,1)}, bf16[2,128,384]{2,1,0:T(8,128)(2,1)}, u32[]{:S(2)}, u32[]{:S(2)}) collective-permute-start(bf16[2,128,384]{2,1,0:T(8,128)(2,1)} %gather_fusion), channel_id=1, source_target_pairs={{0,63},{1,0},{2,1},{3,2},{4,3},{5,4},{6,5},{7,6},{8,7},{9,8},{10,9... | collective-permute-start | bytes 589832 | tf_op jit(solution)/shard_map/ppermute | solution.py:14
  19.1 9.9 %collective-permute-start.4 = (bf16[1,128,512]{2,1,0:T(8,128)(2,1)}, bf16[1,128,512]{2,1,0:T(8,128)(2,1)S(1)}, u32[]{:S(2)}, u32[]{:S(2)}) collective-permute-start(bf16[1,128,512]{2,1,0:T(8,128)(2,1)} %bitcast.59), channel_id=1, source_target_pairs={{0,1},{1,2},{2,3},{3,4},{4,5},{5,6},{6,7},{7,8},{8,9},{9,10},{10,1... | collective-permute-start | bytes 393224 | tf_op jit(solution)/shard_map/ppermute | solution.py:14
  22.8 10.1 %collective-permute-start.5 = (bf16[1,128,512]{2,1,0:T(8,128)(2,1)}, bf16[1,128,512]{2,1,0:T(8,128)(2,1)S(1)}, u32[]{:S(2)}, u32[]{:S(2)}) collective-permute-start(bf16[1,128,512]{2,1,0:T(8,128)(2,1)} %bitcast.60), channel_id=1, source_target_pairs={{0,2},{1,3},{2,4},{3,5},{4,6},{5,7},{6,8},{7,9},{8,10},{9,11},{10,... | collective-permute-start | bytes 393224 | tf_op jit(solution)/shard_map/ppermute | solution.py:14
  29.0 7.8 %collective-permute-start.6 = (bf16[1,128,512]{2,1,0:T(8,128)(2,1)S(1)}, bf16[1,128,512]{2,1,0:T(8,128)(2,1)S(1)}, u32[]{:S(2)}, u32[]{:S(2)}) collective-permute-start(bf16[1,128,512]{2,1,0:T(8,128)(2,1)S(1)} %bitcast.61), channel_id=1, source_target_pairs={{0,63},{1,0},{2,1},{3,2},{4,3},{5,4},{6,5},{7,6},{8,7},{9,8},{10,9... | collective-permute-start | bytes 393224 | tf_op jit(solution)/shard_map/ppermute | solution.py:14
  32.9 10.0 %collective-permute-start.7 = (bf16[1,128,512]{2,1,0:T(8,128)(2,1)S(1)}, bf16[1,128,512]{2,1,0:T(8,128)(2,1)S(1)}, u32[]{:S(2)}, u32[]{:S(2)}) collective-permute-start(bf16[1,128,512]{2,1,0:T(8,128)(2,1)S(1)} %bitcast.62), channel_id=1, source_target_pairs={{0,62},{1,63},{2,0},{3,1},{4,2},{5,3},{6,4},{7,5},{8,6},{9,7},{10,... | collective-permute-start | bytes 393224 | tf_op jit(solution)/shard_map/ppermute | solution.py:14
  36.9 15.7 %collective-permute-start.3 = (bf16[2,128,384]{2,1,0:T(8,128)(2,1)}, bf16[2,128,384]{2,1,0:T(8,128)(2,1)}, u32[]{:S(2)}, u32[]{:S(2)}) collective-permute-start(bf16[2,128,384]{2,1,0:T(8,128)(2,1)} %gather_fusion), channel_id=1, source_target_pairs={{0,62},{1,63},{2,0},{3,1},{4,2},{5,3},{6,4},{7,5},{8,6},{9,7},{10,... | collective-permute-start | bytes 589832 | tf_op jit(solution)/shard_map/ppermute | solution.py:14
  43.6 4.1 copy-start.1
  56.8 1.0 copy-start.8
  57.5 3.5 copy-start.3
  57.5 1.4 copy-start.5
  57.5 1.5 copy-start.12
  59.0 2.0 copy-start.7
  61.0 0.7 copy-start.13
  61.7 5.8 %copy-start.6 = (bf16[1024,512]{1,0:T(8,128)(2,1)}, bf16[1024,512]{1,0:T(8,128)(2,1)S(1)}, u32[]{:S(2)}) copy-start(bf16[1024,512]{1,0:T(8,128)(2,1)S(1)} %convolution_convert_fusion.1) | copy-start | bytes 3145732
  67.5 3.8 copy-start.4
  70.4 1.0 copy-start.15
  71.3 3.9 copy-start.14
  72.7 129.9 %all-reduce.11.cloned.1.call-start = ((), (), s32[]{:S(2)}) async-start(), calls=%async_computation.2 | async-start | bytes 2424832 | tf_op jit(solution)/shard_map/psum | solution.py:110
  76.5 6.1 %copy-start.2 = (bf16[16,128,512]{2,1,0:T(8,128)(2,1)S(1)}, bf16[16,128,512]{2,1,0:T(8,128)(2,1)}, u32[]{:S(2)}) copy-start(bf16[16,128,512]{2,1,0:T(8,128)(2,1)} %copy-done.1) | copy-start | bytes 6291460
  86.3 323.3 %all-reduce.9.cloned.1.call-start = ((), (), s32[]{:S(2)}) async-start(), calls=%async_computation.1 | async-start | bytes 3014656
Sparse Core Ops, SparseCore 0:
  72.8 46.8 all-gather.2
  122.3 80.2 all-reduce.10
  206.4 203.1 all-reduce.8
